TPU v7x, 32 devices: a whole 2x2x4 slice. The times are simulated.
32 devices in a mesh: freq: 4 (over x, core), tile: 8 (over z, y).
Axes of the slice: x: 2, y: 2, z: 4, core: 2. Of those that a mesh axis runs over, the one named last changes fastest.
Arguments:
- travel_time: float32 [512, 8, 512], P('tile', None, 'freq'), may hold values from 0 to 4
- crossing: int32 [8, 512], P('tile'), may hold values from 0 to 63
- bins: int32 [4], P('freq'), may hold values from 8 to 71
- transmission: float32 [4, 2, 64], P('freq'), may hold values from -1 to 1
- capture: bfloat16 [4, 2, 512, 512], P('freq', None, 'tile'), may hold values from -0.01171875 to 0.01171875
Outputs:
- image: float32 [2, 8, 512], P(None, 'tile')
All inputs are finite; a program needn't handle non-finite values.
Results may differ from a plain program's by a relative error of at most 0.0033.
Values may be sent and summed in bfloat16 or wider, within the bound.
No kernel may reach another device: no remote copies, remote signals or barrier semaphores. Data moves between devices by JAX's collectives and lax.ppermute only.
A program may use at most 64 MiB of HBM per device.

v0:
```python
import math
import jax
import jax.numpy as jnp
from jax import lax
from jax.sharding import PartitionSpec as P

TWO_PI = 2.0 * math.pi


def make_fields(times, bin_values):
    scaled = (TWO_PI * bin_values.astype(jnp.float32)).reshape((-1,) + (1,) * times.ndim)
    angle = scaled * times[None]
    return jnp.stack(
        [jnp.cos(angle).astype(jnp.bfloat16), (-jnp.sin(angle)).astype(jnp.bfloat16)], axis=1
    )


def body(travel_time, crossing, bins, transmission, capture):
    group = 1
    senders = lax.axis_size("freq")
    sub = lax.axis_index("freq") % group
    regrouped = lax.all_to_all(travel_time, "tile", split_axis=1, concat_axis=0, tiled=True)
    tile_view = lax.all_gather(regrouped, "freq", axis=2, tiled=True)
    fields = make_fields(tile_view, bins)
    count = fields.shape[0]
    elements = fields.shape[2]
    voxels = fields.shape[3] * fields.shape[4]
    flat = fields.reshape(count, 2, elements, voxels)
    stacked = flat.reshape(count, 2 * elements, voxels)
    piece = lax.all_gather(capture, "tile", axis=2, tiled=True)
    rows = piece.shape[2]
    cap_real = piece[0, 0]
    cap_imag = piece[0, 1]
    block = jnp.concatenate(
        [
            jnp.concatenate([cap_real, -cap_imag], axis=1),
            jnp.concatenate([cap_imag, cap_real], axis=1),
        ],
        axis=0,
    )
    product = jnp.dot(block, stacked[0], preferred_element_type=jnp.float32)
    w_real = product[:rows]
    w_imag = product[rows:]
    g_real = flat[0, 0].astype(jnp.float32)
    g_imag = flat[0, 1].astype(jnp.float32)
    sums_real = [jnp.sum(g_real * w_real - g_imag * w_imag, axis=0)]
    sums_imag = [jnp.sum(g_real * w_imag + g_imag * w_real, axis=0)]
    focus_real = jnp.stack(sums_real)
    focus_imag = jnp.stack(sums_imag)
    row_count = crossing.shape[0]
    columns = crossing.shape[1]
    width = columns // (senders * group)
    cross_view = crossing.reshape(row_count, senders, group, width)
    flat_cross = lax.dynamic_index_in_dim(cross_view, sub, 2, keepdims=False).reshape(-1)
    cells = transmission.shape[2]
    match = flat_cross[None, :] == lax.broadcasted_iota(jnp.int32, (cells, 1), 0)
    coeff_real = jnp.sum(
        jnp.where(match[None], transmission[:, 0][:, :, None], jnp.float32(0.0)), axis=1
    )
    coeff_imag = jnp.sum(
        jnp.where(match[None], transmission[:, 1][:, :, None], jnp.float32(0.0)), axis=1
    )
    square_real = coeff_real * coeff_real - coeff_imag * coeff_imag
    square_imag = 2.0 * coeff_real * coeff_imag
    part_real = jnp.sum(square_real * focus_real - square_imag * focus_imag, axis=0)
    part_imag = jnp.sum(square_real * focus_imag + square_imag * focus_real, axis=0)
    local_part = jnp.stack([part_real, part_imag]).reshape(2, row_count, senders, 1, width)
    selector = (lax.broadcasted_iota(jnp.int32, (1, 1, 1, group, 1), 3) == sub).astype(jnp.float32)
    partial_image = (local_part * selector).reshape(2, row_count, columns)
    image = lax.psum(partial_image, "freq")
    return image


def solution(mesh):
    in_specs = (
        P("tile", None, "freq"),
        P("tile", None),
        P("freq"),
        P("freq", None, None),
        P("freq", None, "tile", None),
    )
    out_specs = P(None, "tile", None)
    return jax.shard_map(body, mesh=mesh, in_specs=in_specs, out_specs=out_specs, check_vma=False)
```

profile of v0, /device:TPU:0, one launch (start us, length us, event | category | flops | bytes accessed | tf_op | source)
XLA Modules:
  0.0 89.6 jit_solution(9563920641388800474)
XLA Ops:
  6.5 0.0 all-gather.5.cloned.1.call-start
  6.5 0.7 all-gather.5.cloned.1.call-update
  7.3 0.0 all-gather.3.cloned.1.call-start
  7.3 1.0 %copy.10 = f32[64,8,128]{2,0,1:T(8,128)S(1)} copy(f32[64,8,128]{2,1,0:T(8,128)} %param.5) | data formatting | bytes 524288 | tf_op args[0]
  8.3 17.1 %all_to_all.18 = f32[64,8,128]{2,0,1:T(8,128)} all-to-all(f32[64,8,128]{2,0,1:T(8,128)S(1)} %copy.10), channel_id=1, replica_groups=mesh['freq'=4,'tile'=8] {'tile'}, dimensions={1} | all-to-all | bytes 524288 | tf_op jit(solution)/shard_map/all_to_all | solution.py:22
  25.4 0.0 all-gather.3.cloned.1.call-update
  26.1 0.8 slice_bitcast_fusion.4
  26.8 0.8 select_reduce_fusion.1
  27.6 24.9 %all-gather.5.cloned.1.call-done = bf16[1,2,512,512]{3,2,1,0:T(8,128)(2,1)} async-done(((bf16[1,2,64,512]{3,2,1,0:T(8,128)(2,1)}), bf16[1,2,512,512]{3,2,1,0:T(8,128)(2,1)}) %all-gather.5.cloned.1.call-update) | async-done | bytes 1048592 | tf_op jit(solution)/shard_map/all_gather | solution.py:30
  52.6 1.1 %fusion.15 = bf16[512,512]{1,0:T(8,128)(2,1)S(1)} fusion(bf16[1,2,512,512]{3,2,1,0:T(8,128)(2,1)} %all-gather.5.cloned.1.call-done), kind=kLoop, calls=%fused_computation.36 | loop fusion | flops 262144 | bytes 1048576 | tf_op jit(solution)/shard_map/neg | solution.py:36
  53.7 1.3 %slice_bitcast_fusion.1 = (bf16[512,512]{1,0:T(8,128)(2,1)S(1)}, bf16[512,512]{1,0:T(8,128)(2,1)S(1)}) fusion(bf16[1,2,512,512]{3,2,1,0:T(8,128)(2,1)} %all-gather.5.cloned.1.call-done), kind=kLoop, calls=%fused_computation.22 | loop fusion | bytes 2097152 | tf_op jit(solution)/shard_map/squeeze | solution.py:33
  54.9 14.8 %all-gather.3.cloned.1.call-done = f32[512,1,512]{2,0,1:T(8,128)} async-done(((f32[512,1,128]{2,0,1:T(8,128)}), f32[512,1,512]{2,0,1:T(8,128)}) %all-gather.3.cloned.1.call-update) | async-done | bytes 1048592 | tf_op jit(solution)/shard_map/all_gather | solution.py:23
  69.7 4.7 %fusion.12 = (bf16[1,1,512,1,512]{4,2,1,3,0:T(8,128)(2,1)S(1)}, bf16[1,1,512,1,512]{4,2,1,3,0:T(8,128)(2,1)S(1)}) fusion(f32[512,1,512]{2,0,1:T(8,128)} %all-gather.3.cloned.1.call-done, f32[]{:T(128)} %bitcast.3), kind=kLoop, calls=%fused_computation.19 | loop fusion | flops 1048576 | bytes 2097156 | tf_op jit(solution)/shard_map/convert_element_type | solution.py:14
  74.5 0.1 fusion.16
  74.6 1.2 %fusion = f32[1024,512]{1,0:T(8,128)S(1)} fusion(bf16[1024,512]{1,0:T(8,128)(2,1)S(1)} %bitcast.43, bf16[512,512]{1,0:T(8,128)(2,1)S(1)} %get-tuple-element.12, bf16[512,512]{1,0:T(8,128)(2,1)S(1)} %get-tuple-element.11, bf16[512,512]{1,0:T(8,128)(2,1)S(1)} %fusion.15), kind=kOutput, calls=%fused_computation | convolution fusion | flops 1082130432 | bytes 4718592 | tf_op jit(solution)/shard_map/dot_general | solution.py:41
  75.9 0.4 fusion.11
  76.3 6.5 %psum.7 = f32[2,1,512]{2,1,0:T(1,128)} all-reduce(f32[2,1,512]{2,1,0:T(1,128)S(1)} %pad_maximum_fusion.1), channel_id=1, replica_groups=mesh['freq'=4,'tile'=8] {'freq'}, use_global_device_ids=true, to_apply=%region_4.5 | all-reduce | flops 1024 | bytes 8192 | tf_op jit(solution)/shard_map/psum | solution.py:70
  (2 shorter events, 0.0 us)
Async XLA Ops:
  6.5 46.0 %all-gather.5.cloned.1.call-start = ((), (), s32[]{:S(2)}) async-start(), calls=%async_computation.2 | async-start | bytes 1179648 | tf_op jit(solution)/shard_map/all_gather | solution.py:30
  7.3 62.5 %all-gather.3.cloned.1.call-start = ((), (), s32[]{:S(2)}) async-start(), calls=%async_computation.1 | async-start | bytes 1310720 | tf_op jit(solution)/shard_map/all_gather | solution.py:23
Sparse Core Ops, SparseCore 0:
  9.5 42.9 all-gather.4
  54.1 15.5 all-gather.2
where the time goes:
time: 90 us; the launch traced here: 89.6 us
  waiting for transfers between devices  40.5 us (45%)
  blocking collectives  23.6 us (26%)
  between operations  14.1 us (16%)
  other arithmetic  7.14 us (8%)
  local copies, waits for them, and re-layouts  3.03 us (3%)
  matrix products  1.24 us (1%)
    all_gather x1, waiting for transfers between devices, body(): piece = lax.all_gather(capture, 'tile', axis=2, tiled=True)  24.9 us
    all_to_all x1, blocking collectives, body(): lax.all_to_all(travel_time, 'tile', split_axis=1, concat_axis=0, tiled=True)  17.1 us
    all_gather x1, waiting for transfers between devices, body(): tile_view = lax.all_gather(regrouped, 'freq', axis=2, tiled=True)  14.8 us
    psum x1, blocking collectives, body(): image = lax.psum(partial_image, 'freq')  6.49 us
    convert_element_type x1, other arithmetic, make_fields(): jnp.cos(angle).astype(jnp.bfloat16)  4.75 us
  transfers between devices with their start and end apart: 2, of which 2 were waited for; matrix products, arithmetic and copies ran while one was open for 5% of the time, Pallas kernels for 0%

commit v1 on v0

--- a/solution.py
+++ b/solution.py
@@ -5,6 +5,22 @@
 from jax.sharding import PartitionSpec as P
 
 TWO_PI = 2.0 * math.pi
+
+
+def pairwise_exchange(x, axis, split, join):
+    ways, here = (lax.axis_size(axis), lax.axis_index(axis))
+    width = x.shape[split] // ways
+    shape = list(x.shape)
+    shape[split] = width
+    height = shape[join]
+    shape[join] = height * ways
+    full = jnp.zeros(shape, x.dtype)
+    for mask in range(ways):
+        part = lax.dynamic_slice_in_dim(x, (here ^ mask) * width, width, axis=split)
+        if mask:
+            part = lax.ppermute(part, axis, [(d, d ^ mask) for d in range(ways)])
+        full = lax.dynamic_update_slice_in_dim(full, part, (here ^ mask) * height, axis=join)
+    return full
 
 
 def make_fields(times, bin_values):
@@ -19,7 +35,7 @@
     group = 1
     senders = lax.axis_size("freq")
     sub = lax.axis_index("freq") % group
-    regrouped = lax.all_to_all(travel_time, "tile", split_axis=1, concat_axis=0, tiled=True)
+    regrouped = pairwise_exchange(travel_time, "tile", 1, 0)
     tile_view = lax.all_gather(regrouped, "freq", axis=2, tiled=True)
     fields = make_fields(tile_view, bins)
     count = fields.shape[0]

time: 90 us -> 102 us (1.13)
  blocking collectives: 23.6 us -> 6.26 us
  waiting for transfers between devices: 40.5 us -> 56.1 us
  starting transfers between devices: 0.04 us -> 12.7 us
  local copies, waits for them, and re-layouts: 3.03 us -> 5.41 us
  other arithmetic: 7.14 us -> 6.1 us
    all_to_all x1 -> x0, blocking collectives: 17.1 us -> none  [body(): lax.all_to_all(travel_time, 'tile', split_axis=1, concat_axis=0, tiled=True)]
    ppermute x0 -> x7, starting transfers between devices: none -> 12.6 us  [pairwise_exchange(): part = lax.ppermute(part, axis, [(d, d ^ mask) for d in range(ways)])]
    all_gather x1, waiting for transfers between devices: 24.9 us -> 37.5 us  [body(): piece = lax.all_gather(capture, 'tile', axis=2, tiled=True)]
    ppermute x0 -> x7, waiting for transfers between devices: none -> 6.52 us  [pairwise_exchange(): part = lax.ppermute(part, axis, [(d, d ^ mask) for d in range(ways)])]
    all_gather x1, waiting for transfers between devices: 14.8 us -> 11.3 us  [body(): tile_view = lax.all_gather(regrouped, 'freq', axis=2, tiled=True)]
    dynamic_slice x0 -> x1, local copies, waits for them, and re-layouts: none -> 2.33 us  [pairwise_exchange(): part = lax.dynamic_slice_in_dim(x, (here ^ mask) * width, width, axis=split)]
    neg x1, other arithmetic: 1.08 us -> 0.04 us  [body(): -cap_imag]
  transfers between devices with their start and end apart: 2 -> 9, of which waited for: 2 -> 5; matrix products, arithmetic and copies ran while one was open for 5% -> 6% of each run, Pallas kernels for 0% -> 0%
where the time goes in v1:
time: 102 us
  waiting for transfers between devices  56.1 us (55%)
  between operations  14.2 us (14%)
  starting transfers between devices  12.7 us (12%)
  blocking collectives  6.26 us (6%)
  other arithmetic  6.1 us (6%)
  local copies, waits for them, and re-layouts  5.41 us (5%)
  matrix products  1.24 us (1%)
    all_gather x1, waiting for transfers between devices, body(): piece = lax.all_gather(capture, 'tile', axis=2, tiled=True)  37.5 us
    ppermute x7, starting transfers between devices, pairwise_exchange(): part = lax.ppermute(part, axis, [(d, d ^ mask) for d in range(ways)])  12.6 us
    all_gather x1, waiting for transfers between devices, body(): tile_view = lax.all_gather(regrouped, 'freq', axis=2, tiled=True)  11.3 us
    ppermute x7, waiting for transfers between devices, pairwise_exchange(): part = lax.ppermute(part, axis, [(d, d ^ mask) for d in range(ways)])  6.52 us
    psum x1, blocking collectives, body(): image = lax.psum(partial_image, 'freq')  6.26 us
    convert_element_type x1, other arithmetic, make_fields(): jnp.cos(angle).astype(jnp.bfloat16)  4.75 us
    dynamic_slice x1, local copies, waits for them, and re-layouts, pairwise_exchange(): part = lax.dynamic_slice_in_dim(x, (here ^ mask) * width, width, axis=split)  2.33 us
  transfers between devices with their start and end apart: 9, of which 5 were waited for; matrix products, arithmetic and copies ran while one was open for 6% of the time, Pallas kernels for 0%

profile of v1, /device:TPU:0, one launch (start us, length us, event | category | flops | bytes accessed | tf_op | source)
XLA Modules:
  0.0 102.0 jit_solution(10711877816600140733)
XLA Ops:
  6.5 0.0 all-gather.3.cloned.1.call-start
  6.5 2.3 %constant_dynamic-slice_fusion = (f32[64,1,128]{2,1,0:T(1,128)S(1)}, f32[64,1,128]{2,1,0:T(1,128)S(1)}, f32[64,1,128]{2,1,0:T(1,128)S(1)}, f32[64,1,128]{2,1,0:T...) fusion(f32[64,8,128]{2,1,0:T(8,128)} %param.5, ...), kind=kLoop, calls=%fused_computation.30 | loop fusion | bytes 524320 | tf_op jit(solution)/shard_map/dynamic_slice | solution.py:19
  8.9 3.0 %collective-permute-start = (f32[64,1,128]{2,0,1:T(8,128)S(1)}, f32[64,1,128]{2,0,1:T(8,128)S(1)}, u32[]{:S(2)}, u32[]{:S(2)}) collective-permute-start(f32[64,1,128]{2,0,1:T(8,128)S(1)} %bitcast.54), channel_id=1, source_target_pairs={{0,1},{1,0},{2,3},{3,2},{4,5},{5,4},{6,7},{7,6},{8,9},{9,8},{10,11... | collective-permute-start | bytes 98312 | tf_op jit(solution)/shard_map/ppermute | solution.py:21
  11.9 1.6 %collective-permute-start.1 = (f32[64,1,128]{2,0,1:T(8,128)S(1)}, f32[64,1,128]{2,0,1:T(8,128)S(1)}, u32[]{:S(2)}, u32[]{:S(2)}) collective-permute-start(f32[64,1,128]{2,0,1:T(8,128)S(1)} %bitcast.53), channel_id=1, source_target_pairs={{0,2},{1,3},{2,0},{3,1},{4,6},{5,7},{6,4},{7,5},{8,10},{9,11},{10,... | collective-permute-start | bytes 98312 | tf_op jit(solution)/shard_map/ppermute | solution.py:21
  13.5 0.0 collective-permute-start.2
  13.5 3.0 %collective-permute-start.3 = (f32[64,1,128]{2,0,1:T(8,128)S(1)}, f32[64,1,128]{2,0,1:T(8,128)S(1)}, u32[]{:S(2)}, u32[]{:S(2)}) collective-permute-start(f32[64,1,128]{2,0,1:T(8,128)S(1)} %bitcast.51), channel_id=1, source_target_pairs={{0,4},{1,5},{2,6},{3,7},{4,0},{5,1},{6,2},{7,3},{8,12},{9,13},{10,... | collective-permute-start | bytes 98312 | tf_op jit(solution)/shard_map/ppermute | solution.py:21
  16.5 1.3 %collective-permute-start.4 = (f32[64,1,128]{2,0,1:T(8,128)S(1)}, f32[64,1,128]{2,0,1:T(8,128)S(1)}, u32[]{:S(2)}, u32[]{:S(2)}) collective-permute-start(f32[64,1,128]{2,0,1:T(8,128)S(1)} %bitcast.50), channel_id=1, source_target_pairs={{0,5},{1,4},{2,7},{3,6},{4,1},{5,0},{6,3},{7,2},{8,13},{9,12},{10,... | collective-permute-start | bytes 98312 | tf_op jit(solution)/shard_map/ppermute | solution.py:21
  17.9 0.0 collective-permute-done
  17.9 3.7 %collective-permute-start.5 = (f32[64,1,128]{2,0,1:T(8,128)S(1)}, f32[64,1,128]{2,0,1:T(8,128)S(1)}, u32[]{:S(2)}, u32[]{:S(2)}) collective-permute-start(f32[64,1,128]{2,0,1:T(8,128)S(1)} %bitcast.49), channel_id=1, source_target_pairs={{0,6},{1,7},{2,4},{3,5},{4,2},{5,3},{6,0},{7,1},{8,14},{9,15},{10,... | collective-permute-start | bytes 98312 | tf_op jit(solution)/shard_map/ppermute | solution.py:21
  21.5 0.0 collective-permute-done.1
  21.5 0.1 collective-permute-start.6
  21.6 0.0 collective-permute-done.2
  21.7 0.0 collective-permute-done.3
  21.7 0.5 collective-permute-done.4
  22.2 1.5 %collective-permute-done.5 = f32[64,1,128]{2,0,1:T(8,128)S(1)} collective-permute-done((f32[64,1,128]{2,0,1:T(8,128)S(1)}, f32[64,1,128]{2,0,1:T(8,128)S(1)}, u32[]{:S(2)}, u32[]{:S(2)}) %collective-permute-start.5) | collective-permute-done | bytes 32800 | tf_op jit(solution)/shard_map/ppermute | solution.py:21
  23.7 4.6 %collective-permute-done.6 = f32[64,1,128]{2,0,1:T(8,128)S(1)} collective-permute-done((f32[64,1,128]{2,0,1:T(8,128)S(1)}, f32[64,1,128]{2,0,1:T(8,128)S(1)}, u32[]{:S(2)}, u32[]{:S(2)}) %collective-permute-start.6) | collective-permute-done | bytes 32800 | tf_op jit(solution)/shard_map/ppermute | solution.py:21
  28.2 0.0 copy-start.1
  28.2 0.7 copy-done.1
  28.9 0.0 all-gather.3.cloned.1.call-update
  28.9 0.0 all-gather.5.cloned.1.call-start
  29.0 0.7 all-gather.5.cloned.1.call-update
  30.4 0.8 slice_bitcast_fusion.4
  31.1 0.8 select_reduce_fusion.1
  31.9 11.3 %all-gather.3.cloned.1.call-done = f32[512,1,512]{2,0,1:T(8,128)} async-done(((f32[512,1,128]{2,0,1:T(8,128)}), f32[512,1,512]{2,0,1:T(8,128)}) %all-gather.3.cloned.1.call-update) | async-done | bytes 1048592 | tf_op jit(solution)/shard_map/all_gather | solution.py:39
  43.2 4.7 %fusion.12 = (bf16[1,1,512,1,512]{4,2,1,3,0:T(8,128)(2,1)S(1)}, bf16[1,1,512,1,512]{4,2,1,3,0:T(8,128)(2,1)S(1)}) fusion(f32[512,1,512]{2,0,1:T(8,128)} %all-gather.3.cloned.1.call-done, f32[]{:T(128)} %bitcast.3), kind=kLoop, calls=%fused_computation.19 | loop fusion | flops 1048576 | bytes 2097156 | tf_op jit(solution)/shard_map/convert_element_type | solution.py:30
  48.0 0.1 fusion.16
  48.1 37.5 %all-gather.5.cloned.1.call-done = bf16[1,2,512,512]{3,2,1,0:T(8,128)(2,1)} async-done(((bf16[1,2,64,512]{3,2,1,0:T(8,128)(2,1)}), bf16[1,2,512,512]{3,2,1,0:T(8,128)(2,1)}) %all-gather.5.cloned.1.call-update) | async-done | bytes 1048592 | tf_op jit(solution)/shard_map/all_gather | solution.py:46
  85.6 1.4 %slice_bitcast_fusion.1 = (bf16[512,512]{1,0:T(8,128)(2,1)S(1)}, bf16[512,512]{1,0:T(8,128)(2,1)S(1)}) fusion(bf16[1,2,512,512]{3,2,1,0:T(8,128)(2,1)} %all-gather.5.cloned.1.call-done), kind=kLoop, calls=%fused_computation.22 | loop fusion | bytes 2097152 | tf_op jit(solution)/shard_map/squeeze | solution.py:49
  87.0 0.2 copy-done
  87.2 1.2 %fusion = f32[1024,512]{1,0:T(8,128)S(1)} fusion(bf16[1024,512]{1,0:T(8,128)(2,1)S(1)} %bitcast.46, bf16[512,512]{1,0:T(8,128)(2,1)S(1)} %get-tuple-element.12, bf16[512,512]{1,0:T(8,128)(2,1)S(1)} %get-tuple-element.11, bf16[512,512]{1,0:T(8,128)(2,1)S(1)} %fusion.15), kind=kOutput, calls=%fused_computation | convolution fusion | flops 1082130432 | bytes 4718592 | tf_op jit(solution)/shard_map/dot_general | solution.py:57
  88.4 0.4 fusion.11
  88.9 6.3 %psum.7 = f32[2,1,512]{2,1,0:T(1,128)} all-reduce(f32[2,1,512]{2,1,0:T(1,128)S(1)} %pad_maximum_fusion.1), channel_id=1, replica_groups=mesh['freq'=4,'tile'=8] {'freq'}, use_global_device_ids=true, to_apply=%region_4.5 | all-reduce | flops 1024 | bytes 8192 | tf_op jit(solution)/shard_map/psum | solution.py:86
  (13 shorter events, 0.1 us)
Async XLA Ops:
  6.5 36.7 %all-gather.3.cloned.1.call-start = ((), (), s32[]{:S(2)}) async-start(), calls=%async_computation | async-start | bytes 1310720 | tf_op jit(solution)/shard_map/all_gather | solution.py:39
  8.9 9.0 %collective-permute-start = (f32[64,1,128]{2,0,1:T(8,128)S(1)}, f32[64,1,128]{2,0,1:T(8,128)S(1)}, u32[]{:S(2)}, u32[]{:S(2)}) collective-permute-start(f32[64,1,128]{2,0,1:T(8,128)S(1)} %bitcast.54), channel_id=1, source_target_pairs={{0,1},{1,0},{2,3},{3,2},{4,5},{5,4},{6,7},{7,6},{8,9},{9,8},{10,11... | collective-permute-start | bytes 98312 | tf_op jit(solution)/shard_map/ppermute | solution.py:21
  11.9 9.6 %collective-permute-start.1 = (f32[64,1,128]{2,0,1:T(8,128)S(1)}, f32[64,1,128]{2,0,1:T(8,128)S(1)}, u32[]{:S(2)}, u32[]{:S(2)}) collective-permute-start(f32[64,1,128]{2,0,1:T(8,128)S(1)} %bitcast.53), channel_id=1, source_target_pairs={{0,2},{1,3},{2,0},{3,1},{4,6},{5,7},{6,4},{7,5},{8,10},{9,11},{10,... | collective-permute-start | bytes 98312 | tf_op jit(solution)/shard_map/ppermute | solution.py:21
  13.5 8.2 %collective-permute-start.2 = (f32[64,1,128]{2,0,1:T(8,128)S(1)}, f32[64,1,128]{2,0,1:T(8,128)S(1)}, u32[]{:S(2)}, u32[]{:S(2)}) collective-permute-start(f32[64,1,128]{2,0,1:T(8,128)S(1)} %bitcast.52), channel_id=1, source_target_pairs={{0,3},{1,2},{2,1},{3,0},{4,7},{5,6},{6,5},{7,4},{8,11},{9,10},{10,... | collective-permute-start | bytes 98312 | tf_op jit(solution)/shard_map/ppermute | solution.py:21
  13.5 8.2 %collective-permute-start.3 = (f32[64,1,128]{2,0,1:T(8,128)S(1)}, f32[64,1,128]{2,0,1:T(8,128)S(1)}, u32[]{:S(2)}, u32[]{:S(2)}) collective-permute-start(f32[64,1,128]{2,0,1:T(8,128)S(1)} %bitcast.51), channel_id=1, source_target_pairs={{0,4},{1,5},{2,6},{3,7},{4,0},{5,1},{6,2},{7,3},{8,12},{9,13},{10,... | collective-permute-start | bytes 98312 | tf_op jit(solution)/shard_map/ppermute | solution.py:21
  16.5 5.7 %collective-permute-start.4 = (f32[64,1,128]{2,0,1:T(8,128)S(1)}, f32[64,1,128]{2,0,1:T(8,128)S(1)}, u32[]{:S(2)}, u32[]{:S(2)}) collective-permute-start(f32[64,1,128]{2,0,1:T(8,128)S(1)} %bitcast.50), channel_id=1, source_target_pairs={{0,5},{1,4},{2,7},{3,6},{4,1},{5,0},{6,3},{7,2},{8,13},{9,12},{10,... | collective-permute-start | bytes 98312 | tf_op jit(solution)/shard_map/ppermute | solution.py:21
  17.9 5.8 %collective-permute-start.5 = (f32[64,1,128]{2,0,1:T(8,128)S(1)}, f32[64,1,128]{2,0,1:T(8,128)S(1)}, u32[]{:S(2)}, u32[]{:S(2)}) collective-permute-start(f32[64,1,128]{2,0,1:T(8,128)S(1)} %bitcast.49), channel_id=1, source_target_pairs={{0,6},{1,7},{2,4},{3,5},{4,2},{5,3},{6,0},{7,1},{8,14},{9,15},{10,... | collective-permute-start | bytes 98312 | tf_op jit(solution)/shard_map/ppermute | solution.py:21
  21.5 6.7 %collective-permute-start.6 = (f32[64,1,128]{2,0,1:T(8,128)S(1)}, f32[64,1,128]{2,0,1:T(8,128)S(1)}, u32[]{:S(2)}, u32[]{:S(2)}) collective-permute-start(f32[64,1,128]{2,0,1:T(8,128)S(1)} %bitcast.48), channel_id=1, source_target_pairs={{0,7},{1,6},{2,5},{3,4},{4,3},{5,2},{6,1},{7,0},{8,15},{9,14},{10,... | collective-permute-start | bytes 98312 | tf_op jit(solution)/shard_map/ppermute | solution.py:21
  28.2 0.7 copy-start.1
  28.9 56.7 %all-gather.5.cloned.1.call-start = ((), (), s32[]{:S(2)}) async-start(), calls=%async_computation.1 | async-start | bytes 1179648 | tf_op jit(solution)/shard_map/all_gather | solution.py:46
  85.6 1.5 %copy-start = (bf16[1,2,512,512]{3,2,1,0:T(8,128)(2,1)S(1)}, bf16[1,2,512,512]{3,2,1,0:T(8,128)(2,1)}, u32[]{:S(2)}) copy-start(bf16[1,2,512,512]{3,2,1,0:T(8,128)(2,1)} %all-gather.5.cloned.1.call-done) | copy-start | bytes 3145732
Sparse Core Ops, SparseCore 0:
  29.1 14.0 all-gather.2
  45.4 40.1 all-gather.4
